TPU v7x, 512 devices: a whole 4x4x16 slice. The times are simulated.
512 devices in a mesh: outer: 16 (over z), inner: 32 (over y, x, core).
Axes of the slice: x: 4, y: 4, z: 16, core: 2. Of those that a mesh axis runs over, the one named last changes fastest.
Arguments:
- field_slab: float32 [512, 128, 4096], P(None, 'inner', 'outer'), may hold values from -48 to 48, as said below
- start_block: float32 [512, 256], replicated, may hold values from -6 to 6
Outputs:
- factor: float32 [512, 256], replicated
- core_fibres: float32 [256, 128, 4096], P('inner', None, 'outer')
Inputs may be any that keep to these rules, and one draw needn't show every extreme that they name: `field_slab`: real values.
All inputs are finite; a program needn't handle non-finite values.
Results may differ from a plain program's by a relative error of at most 0.00016.
Values sent between devices are 32-bit elements; how exact they have to be, the bound alone decides.
No kernel may reach another device: no remote copies, remote signals or barrier semaphores. Data moves between devices by JAX's collectives and lax.ppermute only.
A program may use at most 64 MiB of HBM per device.

v0:
```python
import jax
import jax.numpy as jnp
from jax import lax
from jax.sharding import PartitionSpec as P

ITERS = 2


def product(first_mat, second_mat):
    return jnp.dot(
        first_mat, second_mat, precision=lax.Precision.HIGHEST, preferred_element_type=jnp.float32
    )


def orthonormal(block):
    chol_factor = jnp.linalg.cholesky(product(block.T, block))
    return lax.linalg.triangular_solve(
        chol_factor, block, left_side=False, lower=True, transpose_a=True
    )


def on_device(field_slab, start_block):
    order_rows = field_slab.shape[0]
    local_shape = field_slab.shape
    unfolded = field_slab.reshape(order_rows, local_shape[1] * local_shape[2])
    gram_local = product(unfolded, unfolded.T)
    subspace = orthonormal(start_block)
    gram_total = lax.psum(gram_local, ("outer", "inner"))
    for sweep_index in range(ITERS):
        subspace = orthonormal(product(gram_total, subspace))
    core_block = product(subspace.T, unfolded).reshape(
        subspace.shape[1], local_shape[1], local_shape[2]
    )
    core_fibres = lax.all_to_all(core_block, "inner", split_axis=0, concat_axis=1, tiled=True)
    return (subspace, core_fibres)


def solution(mesh):
    in_specs = (P(None, "inner", "outer"), P())
    out_specs = (P(), P("inner", None, "outer"))
    return jax.shard_map(
        on_device, mesh=mesh, in_specs=in_specs, out_specs=out_specs, check_vma=False
    )
```

profile of v0, /device:TPU:1, one launch (start us, length us, event | category | flops | bytes accessed | tf_op | source)
XLA Modules:
  0.0 663.9 jit_solution(16527323154972641272)
XLA Ops:
  7.2 7.2 %fusion.2 = f32[512,512]{1,0:T(8,128)} fusion(f32[512,4,256]{2,1,0:T(4,128)} %param.5), kind=kOutput, calls=%fused_computation.8 | convolution fusion | flops 3221225472 | bytes 3145728 | tf_op jit(solution)/shard_map/dot_general | solution.py:10
  14.4 1.0 fusion.52
  15.7 11.7 %cholesky.172 = f32[128,128]{1,0:T(8,128)S(1)} custom-call(f32[128,128]{1,0:T(8,128)S(1)} %cholesky.270), custom_call_target="Cholesky" | custom-call | tf_op jit(solution)/shard_map/jit(cholesky)/cholesky | solution.py:16
  27.4 9.8 %custom-call.15 = f32[1,128,128]{1,2,0:T(8,128)S(1)} custom-call(f32[1,128,128]{2,1,0:T(8,128)S(1)} %get-tuple-element.72), custom_call_target="InvertDiagBlocksLowerTriangular" | custom-call | tf_op jit(solution)/shard_map/jit(cholesky)/cholesky | solution.py:16
  37.7 12.0 %cholesky.189 = f32[128,128]{1,0:T(8,128)S(1)} custom-call(f32[128,128]{1,0:T(8,128)S(1)} %convolution_subtract_fusion.5), custom_call_target="Cholesky" | custom-call | tf_op jit(solution)/shard_map/jit(cholesky)/cholesky | solution.py:16
  49.7 0.7 compare_reduce_fusion.4
  51.7 3.8 while.6
  52.3 1.3 bitcast_dynamic-update-slice_fusion.6
  54.2 1.3 bitcast_dynamic-update-slice_fusion.6
  55.5 19.7 %custom-call.16 = f32[2,128,128]{1,2,0:T(8,128)S(1)} custom-call(f32[2,128,128]{2,1,0:T(8,128)S(1)} %get-tuple-element.24), custom_call_target="InvertDiagBlocksLowerTriangular" | custom-call | tf_op jit(solution)/shard_map/triangular_solve/custom-call.0 | solution.py:17
  75.6 1.8 copy.21
  77.4 1.9 copy.17
  79.4 0.6 convolution_subtract_fusion.2
  80.4 406.9 %all-reduce.3.cloned.1.call-done = f32[512,512]{1,0:T(8,128)} async-done(((f32[512,512]{1,0:T(8,128)}), f32[512,512]{1,0:T(8,128)}) %all-reduce.3.cloned.1.call-update) | async-done | bytes 1048592 | tf_op jit(solution)/shard_map/psum | solution.py:28
  487.3 2.2 fusion.5
  489.5 1.0 fusion.53
  490.8 11.7 %cholesky.206 = f32[128,128]{1,0:T(8,128)S(1)} custom-call(f32[128,128]{1,0:T(8,128)S(1)} %cholesky.273), custom_call_target="Cholesky" | custom-call | tf_op jit(solution)/shard_map/jit(cholesky)/cholesky | solution.py:16
  502.5 9.8 %custom-call.17 = f32[1,128,128]{1,2,0:T(8,128)S(1)} custom-call(f32[1,128,128]{2,1,0:T(8,128)S(1)} %get-tuple-element.68), custom_call_target="InvertDiagBlocksLowerTriangular" | custom-call | tf_op jit(solution)/shard_map/jit(cholesky)/cholesky | solution.py:16
  512.8 22.6 %cholesky.223 = f32[128,128]{1,0:T(8,128)S(1)} custom-call(f32[128,128]{1,0:T(8,128)S(1)} %convolution_subtract_fusion.4), custom_call_target="Cholesky" | custom-call | tf_op jit(solution)/shard_map/jit(cholesky)/cholesky | solution.py:16
  535.5 0.7 compare_reduce_fusion.2
  536.2 0.6 compare_reduce_fusion.3
  538.2 4.1 while.7
  538.3 0.6 fusion.80
  538.9 1.4 bitcast_dynamic-update-slice_fusion.7
  540.3 0.6 fusion.80
  540.9 1.4 bitcast_dynamic-update-slice_fusion.7
  542.4 19.7 %custom-call.18 = f32[2,128,128]{1,2,0:T(8,128)S(1)} custom-call(f32[2,128,128]{2,1,0:T(8,128)S(1)} %get-tuple-element.25), custom_call_target="InvertDiagBlocksLowerTriangular" | custom-call | tf_op jit(solution)/shard_map/triangular_solve/custom-call.0 | solution.py:17
  562.5 0.6 convolution_subtract_fusion.1
  563.5 1.0 fusion.9
  564.5 1.0 fusion.54
  565.8 11.7 %cholesky.240 = f32[128,128]{1,0:T(8,128)S(1)} custom-call(f32[128,128]{1,0:T(8,128)S(1)} %cholesky.276), custom_call_target="Cholesky" | custom-call | tf_op jit(solution)/shard_map/jit(cholesky)/cholesky | solution.py:16
  577.5 9.8 %custom-call.19 = f32[1,128,128]{1,2,0:T(8,128)S(1)} custom-call(f32[1,128,128]{2,1,0:T(8,128)S(1)} %get-tuple-element.64), custom_call_target="InvertDiagBlocksLowerTriangular" | custom-call | tf_op jit(solution)/shard_map/jit(cholesky)/cholesky | solution.py:16
  587.8 11.9 %cholesky.257 = f32[128,128]{1,0:T(8,128)S(1)} custom-call(f32[128,128]{1,0:T(8,128)S(1)} %convolution_subtract_fusion.3), custom_call_target="Cholesky" | custom-call | tf_op jit(solution)/shard_map/jit(cholesky)/cholesky | solution.py:16
  599.8 0.7 compare_reduce_fusion
  600.5 0.6 compare_reduce_fusion.1
  602.5 4.1 while.8
  602.5 0.6 fusion.81
  603.1 1.4 bitcast_dynamic-update-slice_fusion.8
  604.6 0.6 fusion.81
  605.2 1.4 bitcast_dynamic-update-slice_fusion.8
  606.6 19.7 %custom-call.20 = f32[2,128,128]{1,2,0:T(8,128)S(1)} custom-call(f32[2,128,128]{2,1,0:T(8,128)S(1)} %get-tuple-element.26), custom_call_target="InvertDiagBlocksLowerTriangular" | custom-call | tf_op jit(solution)/shard_map/triangular_solve/custom-call.0 | solution.py:17
  626.7 0.6 convolution_subtract_fusion
  627.8 1.9 fusion.13
  629.7 1.6 copy.18
  631.3 6.6 %all-to-all-start = ((f32[256,4,256]{2,1,0:T(4,128)}), f32[256,4,256]{2,1,0:T(4,128)S(1)}, u32[]{:S(2)}, u32[]{:S(2)}) async-start(f32[256,4,256]{2,1,0:T(4,128)} %copy.18), calls=%async_computation | async-start | bytes 2097152 | tf_op jit(solution)/shard_map/all_to_all | solution.py:34
  638.0 1.0 copy.20
  639.0 16.1 %all-to-all-done = f32[256,4,256]{2,1,0:T(4,128)S(1)} async-done(((f32[256,4,256]{2,1,0:T(4,128)}), f32[256,4,256]{2,1,0:T(4,128)S(1)}, u32[]{:S(2)}, u32[]{:S(2)}) %all-to-all-start) | async-done | bytes 1048608 | tf_op jit(solution)/shard_map/all_to_all | solution.py:34
  655.4 1.3 all_to_all.16
  (56 shorter events, 6.4 us)
Async XLA Ops:
  7.2 7.2 %copy-start = (f32[512,256]{1,0:T(8,128)S(1)}, f32[512,256]{1,0:T(8,128)}, u32[]{:S(2)}) copy-start(f32[512,256]{1,0:T(8,128)} %param.6) | copy-start | bytes 1572868
  7.2 480.1 %all-reduce.3.cloned.1.call-start = ((), (), s32[]{:S(2)}) async-start(), calls=%async_computation.1 | async-start | bytes 2097152 | tf_op jit(solution)/shard_map/psum | solution.py:28
  15.6 60.0 %copy-start.2 = (f32[512,4,256]{2,1,0:T(4,128)S(1)}, f32[512,4,256]{2,1,0:T(4,128)}, u32[]{:S(2)}) copy-start(f32[512,4,256]{2,1,0:T(4,128)} %param.5) | copy-start | bytes 6291460
  562.0 1.4 copy-start.1
  631.3 23.8 %all-to-all-start = ((f32[256,4,256]{2,1,0:T(4,128)}), f32[256,4,256]{2,1,0:T(4,128)S(1)}, u32[]{:S(2)}, u32[]{:S(2)}) async-start(f32[256,4,256]{2,1,0:T(4,128)} %copy.18), calls=%async_computation | async-start | bytes 2097152 | tf_op jit(solution)/shard_map/all_to_all | solution.py:34
Sparse Core Ops, SparseCore 0:
  14.5 472.7 all-reduce.2
where the time goes:
time: 673 us; the launch traced here: 664 us
  waiting for transfers between devices  423 us (63%)
  other arithmetic  174 us (26%)
  matrix products  21.1 us (3%)
  local copies, waits for them, and re-layouts  20.3 us (3%)
  between operations  18.7 us (3%)
    psum x1, waiting for transfers between devices, on_device(): gram_total = lax.psum(gram_local, ('outer', 'inner'))  407 us
    another operation x20, other arithmetic, orthonormal(): chol_factor = jnp.linalg.cholesky(product(block.T, block))  115 us
    another operation x8, other arithmetic, orthonormal(): lax.linalg.triangular_solve(chol_factor, block, left_side=False, lower=Tr...  59.2 us
    all_to_all x1, waiting for transfers between devices, on_device(): lax.all_to_all(core_block, 'inner', split_axis=0, concat_axis=1, tiled=True)  16.1 us
    dot_general x7, matrix products, product(): jnp.dot(first_mat, second_mat, precision=lax.Precision.HIGHEST, preferred...  15.4 us
  transfers between devices with their start and end apart: 2, of which 2 were waited for; matrix products, arithmetic and copies ran while one was open for 10% of the time, Pallas kernels for 0%

commit v1 on v0

--- a/solution.py
+++ b/solution.py
@@ -25,7 +25,7 @@
     unfolded = field_slab.reshape(order_rows, local_shape[1] * local_shape[2])
     gram_local = product(unfolded, unfolded.T)
     subspace = orthonormal(start_block)
-    gram_total = lax.psum(gram_local, ("outer", "inner"))
+    gram_total = lax.psum(lax.psum(gram_local, "outer"), "inner")
     for sweep_index in range(ITERS):
         subspace = orthonormal(product(gram_total, subspace))
     core_block = product(subspace.T, unfolded).reshape(

time: 673 us -> 464 us (0.69)
  waiting for transfers between devices: 423 us -> 231 us
  other arithmetic: 174 us -> 163 us
    psum x1 -> x2, waiting for transfers between devices: 407 us -> 214 us  [on_device(): gram_total = lax.psum(lax.psum(gram_local, 'outer'), 'inner')]
    another operation x20, other arithmetic: 115 us -> 104 us  [orthonormal(): chol_factor = jnp.linalg.cholesky(product(block.T, block))]
  transfers between devices with their start and end apart: 2 -> 3, of which waited for: 2 -> 3; matrix products, arithmetic and copies ran while one was open for 10% -> 14% of each run, Pallas kernels for 0% -> 0%
where the time goes in v1:
time: 464 us; the launch traced here: 460 us
  waiting for transfers between devices  231 us (50%)
  other arithmetic  163 us (35%)
  matrix products  21.1 us (5%)
  local copies, waits for them, and re-layouts  20.3 us (4%)
  between operations  18.5 us (4%)
  starting transfers between devices  6.31 us (1%)
    psum x2, waiting for transfers between devices, on_device(): gram_total = lax.psum(lax.psum(gram_local, 'outer'), 'inner')  214 us
    another operation x20, other arithmetic, orthonormal(): chol_factor = jnp.linalg.cholesky(product(block.T, block))  104 us
    another operation x8, other arithmetic, orthonormal(): lax.linalg.triangular_solve(chol_factor, block, left_side=False, lower=Tr...  59.2 us
    all_to_all x1, waiting for transfers between devices, on_device(): lax.all_to_all(core_block, 'inner', split_axis=0, concat_axis=1, tiled=True)  16.1 us
    dot_general x7, matrix products, product(): jnp.dot(first_mat, second_mat, precision=lax.Precision.HIGHEST, preferred...  15.4 us
    another operation x22, local copies, waits for them, and re-layouts, orthonormal(): lax.linalg.triangular_solve(chol_factor, block, left_side=False, lower=Tr...  11.9 us
  transfers between devices with their start and end apart: 3, of which 3 were waited for; matrix products, arithmetic and copies ran while one was open for 14% of the time, Pallas kernels for 0%

profile of v1, /device:TPU:1, one launch (start us, length us, event | category | flops | bytes accessed | tf_op | source)
XLA Modules:
  0.0 460.1 jit_solution(6431365954701264129)
XLA Ops:
  7.2 7.2 %fusion.2 = f32[512,512]{1,0:T(8,128)} fusion(f32[512,4,256]{2,1,0:T(4,128)} %param.5), kind=kOutput, calls=%fused_computation.8 | convolution fusion | flops 3221225472 | bytes 3145728 | tf_op jit(solution)/shard_map/dot_general | solution.py:10
  14.6 1.0 fusion.52
  15.9 11.7 %cholesky.172 = f32[128,128]{1,0:T(8,128)S(1)} custom-call(f32[128,128]{1,0:T(8,128)S(1)} %cholesky.270), custom_call_target="Cholesky" | custom-call | tf_op jit(solution)/shard_map/jit(cholesky)/cholesky | solution.py:16
  27.6 9.8 %custom-call.15 = f32[1,128,128]{1,2,0:T(8,128)S(1)} custom-call(f32[1,128,128]{2,1,0:T(8,128)S(1)} %get-tuple-element.72), custom_call_target="InvertDiagBlocksLowerTriangular" | custom-call | tf_op jit(solution)/shard_map/jit(cholesky)/cholesky | solution.py:16
  37.9 11.7 %cholesky.189 = f32[128,128]{1,0:T(8,128)S(1)} custom-call(f32[128,128]{1,0:T(8,128)S(1)} %convolution_subtract_fusion.5), custom_call_target="Cholesky" | custom-call | tf_op jit(solution)/shard_map/jit(cholesky)/cholesky | solution.py:16
  49.7 0.7 compare_reduce_fusion.4
  51.7 4.2 while.6
  52.7 1.3 bitcast_dynamic-update-slice_fusion.6
  54.6 1.3 bitcast_dynamic-update-slice_fusion.6
  55.9 19.7 %custom-call.16 = f32[2,128,128]{1,2,0:T(8,128)S(1)} custom-call(f32[2,128,128]{2,1,0:T(8,128)S(1)} %get-tuple-element.24), custom_call_target="InvertDiagBlocksLowerTriangular" | custom-call | tf_op jit(solution)/shard_map/triangular_solve/custom-call.0 | solution.py:17
  75.6 74.3 %all-reduce.4.cloned.1.call-done = f32[512,512]{1,0:T(8,128)} async-done(((f32[512,512]{1,0:T(8,128)}), f32[512,512]{1,0:T(8,128)}) %all-reduce.4.cloned.1.call-update) | async-done | bytes 1048592 | tf_op jit(solution)/shard_map/psum | solution.py:28
  150.3 1.8 copy.21
  152.1 1.9 copy.17
  154.0 0.6 convolution_subtract_fusion.2
  155.1 140.1 %all-reduce.6.cloned.1.call-done = f32[512,512]{1,0:T(8,128)} async-done(((f32[512,512]{1,0:T(8,128)}), f32[512,512]{1,0:T(8,128)}) %all-reduce.6.cloned.1.call-update) | async-done | bytes 1048592 | tf_op jit(solution)/shard_map/psum | solution.py:28
  295.1 2.2 fusion.5
  297.4 1.0 fusion.53
  298.6 11.7 %cholesky.206 = f32[128,128]{1,0:T(8,128)S(1)} custom-call(f32[128,128]{1,0:T(8,128)S(1)} %cholesky.273), custom_call_target="Cholesky" | custom-call | tf_op jit(solution)/shard_map/jit(cholesky)/cholesky | solution.py:16
  310.4 9.8 %custom-call.17 = f32[1,128,128]{1,2,0:T(8,128)S(1)} custom-call(f32[1,128,128]{2,1,0:T(8,128)S(1)} %get-tuple-element.68), custom_call_target="InvertDiagBlocksLowerTriangular" | custom-call | tf_op jit(solution)/shard_map/jit(cholesky)/cholesky | solution.py:16
  320.7 11.9 %cholesky.223 = f32[128,128]{1,0:T(8,128)S(1)} custom-call(f32[128,128]{1,0:T(8,128)S(1)} %convolution_subtract_fusion.4), custom_call_target="Cholesky" | custom-call | tf_op jit(solution)/shard_map/jit(cholesky)/cholesky | solution.py:16
  332.6 0.6 compare_reduce_fusion.2
  333.2 0.7 compare_reduce_fusion.3
  335.2 4.1 while.7
  335.3 0.7 fusion.80
  335.9 1.3 bitcast_dynamic-update-slice_fusion.7
  337.3 0.7 fusion.80
  338.0 1.3 bitcast_dynamic-update-slice_fusion.7
  339.3 19.7 %custom-call.18 = f32[2,128,128]{1,2,0:T(8,128)S(1)} custom-call(f32[2,128,128]{2,1,0:T(8,128)S(1)} %get-tuple-element.25), custom_call_target="InvertDiagBlocksLowerTriangular" | custom-call | tf_op jit(solution)/shard_map/triangular_solve/custom-call.0 | solution.py:17
  360.5 1.0 fusion.9
  361.5 1.0 fusion.54
  362.7 11.7 %cholesky.240 = f32[128,128]{1,0:T(8,128)S(1)} custom-call(f32[128,128]{1,0:T(8,128)S(1)} %cholesky.276), custom_call_target="Cholesky" | custom-call | tf_op jit(solution)/shard_map/jit(cholesky)/cholesky | solution.py:16
  374.5 9.8 %custom-call.19 = f32[1,128,128]{1,2,0:T(8,128)S(1)} custom-call(f32[1,128,128]{2,1,0:T(8,128)S(1)} %get-tuple-element.64), custom_call_target="InvertDiagBlocksLowerTriangular" | custom-call | tf_op jit(solution)/shard_map/jit(cholesky)/cholesky | solution.py:16
  384.8 11.9 %cholesky.257 = f32[128,128]{1,0:T(8,128)S(1)} custom-call(f32[128,128]{1,0:T(8,128)S(1)} %convolution_subtract_fusion.3), custom_call_target="Cholesky" | custom-call | tf_op jit(solution)/shard_map/jit(cholesky)/cholesky | solution.py:16
  396.7 0.7 compare_reduce_fusion
  397.5 0.6 compare_reduce_fusion.1
  399.5 4.1 while.8
  399.5 0.6 fusion.81
  400.1 1.4 bitcast_dynamic-update-slice_fusion.8
  401.6 0.6 fusion.81
  402.2 1.4 bitcast_dynamic-update-slice_fusion.8
  403.6 19.7 %custom-call.20 = f32[2,128,128]{1,2,0:T(8,128)S(1)} custom-call(f32[2,128,128]{2,1,0:T(8,128)S(1)} %get-tuple-element.26), custom_call_target="InvertDiagBlocksLowerTriangular" | custom-call | tf_op jit(solution)/shard_map/triangular_solve/custom-call.0 | solution.py:17
  423.7 0.6 convolution_subtract_fusion
  424.7 1.9 fusion.13
  426.7 1.6 copy.18
  428.3 6.1 %all-to-all-start = ((f32[256,4,256]{2,1,0:T(4,128)}), f32[256,4,256]{2,1,0:T(4,128)S(1)}, u32[]{:S(2)}, u32[]{:S(2)}) async-start(f32[256,4,256]{2,1,0:T(4,128)} %copy.18), calls=%async_computation | async-start | bytes 2097152 | tf_op jit(solution)/shard_map/all_to_all | solution.py:34
  434.4 1.0 copy.20
  435.4 16.1 %all-to-all-done = f32[256,4,256]{2,1,0:T(4,128)S(1)} async-done(((f32[256,4,256]{2,1,0:T(4,128)}), f32[256,4,256]{2,1,0:T(4,128)S(1)}, u32[]{:S(2)}, u32[]{:S(2)}) %all-to-all-start) | async-done | bytes 1048608 | tf_op jit(solution)/shard_map/all_to_all | solution.py:34
  451.7 1.3 all_to_all.16
  (59 shorter events, 7.2 us)
Async XLA Ops:
  7.2 7.5 %copy-start = (f32[512,256]{1,0:T(8,128)S(1)}, f32[512,256]{1,0:T(8,128)}, u32[]{:S(2)}) copy-start(f32[512,256]{1,0:T(8,128)} %param.6) | copy-start | bytes 1572868
  7.2 142.7 %all-reduce.4.cloned.1.call-start = ((), (), s32[]{:S(2)}) async-start(), calls=%async_computation.1 | async-start | bytes 2097152 | tf_op jit(solution)/shard_map/psum | solution.py:28
  14.4 280.8 %all-reduce.6.cloned.1.call-start = ((), (), s32[]{:S(2)}) async-start(), calls=%async_computation.2 | async-start | bytes 2097152 | tf_op jit(solution)/shard_map/psum | solution.py:28
  27.6 122.7 %copy-start.2 = (f32[512,4,256]{2,1,0:T(4,128)S(1)}, f32[512,4,256]{2,1,0:T(4,128)}, u32[]{:S(2)}) copy-start(f32[512,4,256]{2,1,0:T(4,128)} %param.5) | copy-start | bytes 6291460
  359.0 1.5 copy-start.1
  428.3 23.2 %all-to-all-start = ((f32[256,4,256]{2,1,0:T(4,128)}), f32[256,4,256]{2,1,0:T(4,128)S(1)}, u32[]{:S(2)}, u32[]{:S(2)}) async-start(f32[256,4,256]{2,1,0:T(4,128)} %copy.18), calls=%async_computation | async-start | bytes 2097152 | tf_op jit(solution)/shard_map/all_to_all | solution.py:34
Sparse Core Ops, SparseCore 0:
  14.5 135.2 all-reduce.3
  153.4 141.6 all-reduce.5
